TPU v7x, 512 devices: a whole 4x8x8 slice. The times are simulated.
512 devices in a mesh: length: 16 (over z, core), girth: 32 (over x, y).
Axes of the slice: x: 4, y: 8, z: 8, core: 2. Of those that a mesh axis runs over, the one named last changes fastest.
Arguments:
- wave_amplitude: bfloat16 [6, 2048, 65536], P(None, 'length', 'girth'), may hold values from -6 to 6
- load_bank: bfloat16 [65536, 256], P('girth'), may hold values from -0.125 to 0.125
- freq_owner: int32 [1], replicated, may hold values from 0 to 31
- thickness_class: int32 [2048, 8192], P('length', 'girth'), may hold values from 0 to 7
- class_stiffness: float32 [8], replicated, may hold values from 0.5 to 4
- coupling: float32 [6, 6], replicated, may hold values from -0.15 to 2, as said below
- stress_map: float32 [4, 6], replicated, may hold values from -2.5 to 2.5
- psd_weight: float32 [1], replicated, may hold values from 0.5 to 2
- hotspot_tile: int32 [16, 1024], P('length', 'girth'), may hold values from 0 to 127
- hotspot_owner: int32 [16, 1024, 1], P('length', 'girth'), may hold values from 0 to 31; in each aligned block of 32 rows (0 to 31, 32 to 63, ..., all dimensions but the last counted through in order) at most 2 rows name the same one
- prior_moments: float32 [16, 32, 32, 2, 2, 256], P('length', 'girth'), may hold values from 0.1 to 1
Outputs:
- response: float32 [6, 2048, 8192], P(None, 'length', 'girth')
- hotspot_moments: float32 [16, 32, 32, 2, 2, 256], P('length', 'girth')
Inputs may be any that keep to these rules, and one draw needn't show every extreme that they name: `hotspot_owner`: in each device's list of 32 hotspots no owner is named more than 2 times, and in some lists an owner is named exactly 2 times. `coupling`: Symmetric; each diagonal entry is at least 1 and exceeds the sum of the magnitudes of the other entries of its row.
All inputs are finite; a program needn't handle non-finite values.
Results may differ from a plain program's by a relative error of at most 0.0003.
Values may be sent and summed in bfloat16 or wider, within the bound.
No kernel may reach another device: no remote copies, remote signals or barrier semaphores. Data moves between devices by JAX's collectives and lax.ppermute only.
A program may use at most 64 MiB of HBM per device.

v0:
```python
import math
import jax
import jax.numpy as jnp
from jax import lax
from jax.sharding import PartitionSpec as P

SWEEPS = 4
CAP = 2


def spread(block, axis, source):
    block = jnp.where(lax.axis_index(axis) == source, block, jnp.zeros_like(block))
    return lax.psum(block, axis)


def padded_2(block, sides, width):
    for axis, dim in sides:
        count = lax.axis_size(axis)
        forward = [(i, i + 1) for i in range(count - 1)]
        backward = [(target, source) for source, target in forward]
        low = lax.ppermute(
            lax.slice_in_dim(block, block.shape[dim] - width, None, axis=dim), axis, forward
        )
        high = lax.ppermute(lax.slice_in_dim(block, 0, width, axis=dim), axis, backward)
        block = jnp.concatenate([low, block, high], axis=dim)
    return block


def chebyshev_weight(sweep):
    return 1.0 / (1.0 + 0.9 * math.cos(math.pi * (2 * sweep + 1) / (2 * SWEEPS)))


def operate_padded(padded, stiffness, coupling):
    centre = padded[:, 1:-1, 1:-1]
    beside = padded[:, 2:, 1:-1] + padded[:, :-2, 1:-1] + padded[:, 1:-1, 2:] + padded[:, 1:-1, :-2]
    mixing = jnp.einsum("ab,bij->aij", coupling, centre, precision=lax.Precision.HIGHEST)
    return stiffness * (4.0 * centre - beside) + mixing


def square_pairs(values, axis_at):
    first = jnp.take(values, 0, axis=axis_at)
    second = jnp.take(values, 1, axis=axis_at)
    third = jnp.take(values, 2, axis=axis_at)
    fourth = jnp.take(values, 3, axis=axis_at)
    return jnp.stack(
        [first * first + second * second, third * third + fourth * fourth], axis=axis_at
    )


def on_device(
    wave_amplitude,
    load_bank,
    freq_owner,
    thickness_class,
    class_stiffness,
    coupling,
    stress_map,
    psd_weight,
    hotspot_tile,
    hotspot_owner,
    prior_moments,
):
    row_count = wave_amplitude.shape[1]
    girth_cells = load_bank.shape[1]
    mode_count = load_bank.shape[0]
    amplitude = wave_amplitude.reshape(6 * row_count, mode_count)
    root = freq_owner[0]
    factors = spread(load_bank, "girth", root)
    loading = jnp.dot(amplitude, factors, preferred_element_type=jnp.float32)
    loading = loading.reshape(6, row_count, girth_cells)
    stiffness = jnp.zeros((row_count, girth_cells), jnp.float32)
    for level in range(class_stiffness.shape[0]):
        stiffness = stiffness + jnp.where(thickness_class == level, class_stiffness[level], 0.0)
    coupling_diag = jnp.diagonal(coupling)[:, None, None]
    diagonal = 4.0 * stiffness[None] + coupling_diag
    motion = chebyshev_weight(0) * (loading / diagonal)
    for sweep in range(1, SWEEPS):
        padded = padded_2(motion, (("length", 1), ("girth", 2)), 1)
        applied = operate_padded(padded, stiffness, coupling)
        motion = motion + chebyshev_weight(sweep) * ((loading - applied) / diagonal)
    girth_count = lax.axis_size("girth")
    tile_ids = hotspot_tile[0]
    owner_ids = hotspot_owner[0, :, 0]
    listed = owner_ids.shape[0]
    positions = jnp.arange(listed, dtype=jnp.int32)
    matching = owner_ids[:, None] == owner_ids[None, :]
    earlier = positions[None, :] < positions[:, None]
    slot_rank = jnp.sum(jnp.logical_and(matching, earlier).astype(jnp.int32), axis=1)
    target = owner_ids * CAP + slot_rank
    stresses = stiffness[:, None, :] * jnp.einsum(
        "ka,aij->ikj", stress_map, motion, precision=lax.Precision.HIGHEST
    )
    stress_rows = jnp.take(stresses, tile_ids, axis=0)
    outbox = jnp.zeros((girth_count * CAP, 4, girth_cells), jnp.float32).at[target].set(stress_rows)
    outbox = outbox.reshape(girth_count, CAP, 4, girth_cells)
    received = lax.all_to_all(outbox, "girth", split_axis=0, concat_axis=0, tiled=True)
    hotspot_moments = prior_moments + (psd_weight[0] * square_pairs(received, 2))[None, None]
    return (motion, hotspot_moments)


def solution(mesh):
    return jax.shard_map(
        on_device,
        mesh=mesh,
        in_specs=(
            P(None, "length", "girth"),
            P("girth", None),
            P(),
            P("length", "girth"),
            P(),
            P(),
            P(),
            P(),
            P("length", "girth"),
            P("length", "girth", None),
            P("length", "girth", None, None, None, None),
        ),
        out_specs=(P(None, "length", "girth"), P("length", "girth", None, None, None, None)),
        check_vma=False,
    )
```

profile of v0, /device:TPU:264, one launch (start us, length us, event | category | flops | bytes accessed | tf_op | source)
XLA Modules:
  0.0 299.6 jit_solution(5316711973554912137)
XLA Ops:
  10.5 5.3 %broadcast_multiply_fusion.1 = (f32[128,256]{1,0:T(8,128)S(1)}, f32[128,256]{1,0:T(8,128)S(1)}) fusion(f32[]{:T(128)} %bitcast.11, s32[128,256]{1,0:T(8,128)S(1)} %copy-done.6, f32[]{:T(128)} %bitcast.10, f32[]{:T(128)} %bitcast.9, f32[]{:T(128)} %bitcast.8, f32[]{:T(128)} %bitcast.7, f32[]{:T(128)} %bitcast.6, f32[]{:T(128)} %bitcast.5, f32[]{:T(128)} %bitcast.4), kind=kLoop, calls=%fused_computation.85 | loop fusion | flops 786432 | bytes 393248 | tf_op jit(solution)/shard_map/mul | solution.py:75
  15.7 156.9 %all-reduce.2.cloned.1.call-done = bf16[2048,256]{1,0:T(8,128)(2,1)} async-done(((bf16[2048,256]{1,0:T(8,128)(2,1)}), bf16[2048,256]{1,0:T(8,128)(2,1)}) %all-reduce.2.cloned.1.call-update) | async-done | bytes 1048592 | tf_op jit(solution)/shard_map/psum | solution.py:13
  172.7 3.1 %convolution_bitcast_fusion.3 = f32[768,256]{0,1:T(8,128)} fusion(bf16[2048,256]{1,0:T(8,128)(2,1)} %all-reduce.2.cloned.1.call-done, bf16[768,2048]{1,0:T(8,128)(2,1)S(1)} %bitcast.120), kind=kOutput, calls=%fused_computation.22 | convolution fusion | flops 805306368 | bytes 4980736 | tf_op jit(solution)/shard_map/dot_general | solution.py:69
  175.8 2.3 copy.53
  178.1 1.8 broadcast_multiply_fusion
  179.9 1.9 collective-permute-start
  181.8 2.4 collective-permute-start.1
  184.3 3.8 %collective-permute-done.1 = f32[6,1,256]{2,0,1:T(8,128)S(1)} collective-permute-done((f32[6,1,256]{2,0,1:T(8,128)S(1)}, f32[6,1,256]{2,0,1:T(8,128)S(1)}, u32[]{:S(2)}, u32[]{:S(2)}) %collective-permute-start.1) | collective-permute-done | bytes 6176 | tf_op jit(solution)/shard_map/ppermute | solution.py:21
  189.3 1.3 copy.55
  190.6 3.4 %collective-permute-start.2 = (f32[6,130,1]{1,2,0:T(1,128)S(1)}, f32[6,130,1]{1,2,0:T(1,128)S(1)}, u32[]{:S(2)}, u32[]{:S(2)}) collective-permute-start(f32[6,130,1]{1,2,0:T(1,128)S(1)} %copy.55), channel_id=1, source_target_pairs={{1,0},{2,1},{3,2},{4,3},{5,4},{6,5},{7,6},{8,7},{9,8},{10,9},{11,1... | collective-permute-start | bytes 9368 | tf_op jit(solution)/shard_map/ppermute | solution.py:24
  195.3 2.4 collective-permute-start.3
  199.2 1.7 collective-permute-done.3
  202.0 6.4 %fusion.11 = f32[6,128,256]{2,0,1:T(8,128)S(1)} fusion(f32[6,128,256]{2,0,1:T(8,128)} %copy-done.2, f32[6,128,256]{2,1,0:T(8,128)} %bitcast.122, f32[6,130,1]{2,0,1:T(8,128)} %copy.58, f32[6,1,256]{2,0,1:T(8,128)S(1)} %collective-permute-done, f32[6,1,256]{2,0,1:T(8,128)S(1)} %collective-permute-done.1, f32[6,130,1]{2,0,1:T(8,128)} %copy.56, ...), kind=kOutput, calls=%fused_computation.21 | convolution fusion | flops 18284544 | bytes 2640136 | tf_op jit(solution)/shard_map/ab,bij->aij/dot_general | solution.py:36
  208.4 1.9 collective-permute-start.4
  210.4 2.4 collective-permute-start.5
  212.8 3.7 %collective-permute-done.5 = f32[6,1,256]{2,0,1:T(8,128)S(1)} collective-permute-done((f32[6,1,256]{2,0,1:T(8,128)S(1)}, f32[6,1,256]{2,0,1:T(8,128)S(1)}, u32[]{:S(2)}, u32[]{:S(2)}) %collective-permute-start.5) | collective-permute-done | bytes 6176 | tf_op jit(solution)/shard_map/ppermute | solution.py:21
  217.8 1.3 copy.60
  219.1 1.9 collective-permute-start.6
  222.4 3.9 %collective-permute-start.7 = (f32[6,130,1]{1,2,0:T(1,128)S(1)}, f32[6,130,1]{1,2,0:T(1,128)S(1)}, u32[]{:S(2)}, u32[]{:S(2)}) collective-permute-start(f32[6,130,1]{1,2,0:T(1,128)S(1)} %copy.62), channel_id=1, source_target_pairs={{0,1},{1,2},{2,3},{3,4},{4,5},{5,6},{6,7},{7,8},{8,9},{9,10},{10,1... | collective-permute-start | bytes 9368 | tf_op jit(solution)/shard_map/ppermute | solution.py:21
  229.1 6.4 %fusion.7 = f32[6,128,256]{2,0,1:T(8,128)S(1)} fusion(f32[6,128,256]{2,0,1:T(8,128)} %copy-done.5, f32[6,128,256]{2,1,0:T(8,128)} %bitcast.123, f32[6,130,1]{2,0,1:T(8,128)} %copy.63, f32[6,1,256]{2,0,1:T(8,128)S(1)} %collective-permute-done.4, f32[6,1,256]{2,0,1:T(8,128)S(1)} %collective-permute-done.5, f32[6,130,1]{2,0,1:T(8,128)} %copy.61, ...), kind=kOutput, calls=%fused_computation.16 | convolution fusion | flops 18087936 | bytes 2640136 | tf_op jit(solution)/shard_map/ab,bij->aij/dot_general | solution.py:36
  235.5 1.9 collective-permute-start.8
  237.4 2.4 collective-permute-start.9
  239.9 3.7 %collective-permute-done.9 = f32[6,1,256]{2,0,1:T(8,128)S(1)} collective-permute-done((f32[6,1,256]{2,0,1:T(8,128)S(1)}, f32[6,1,256]{2,0,1:T(8,128)S(1)}, u32[]{:S(2)}, u32[]{:S(2)}) %collective-permute-start.9) | collective-permute-done | bytes 6176 | tf_op jit(solution)/shard_map/ppermute | solution.py:21
  246.2 1.9 collective-permute-start.10
  249.4 4.1 %collective-permute-start.11 = (f32[6,130,1]{1,2,0:T(1,128)S(1)}, f32[6,130,1]{1,2,0:T(1,128)S(1)}, u32[]{:S(2)}, u32[]{:S(2)}) collective-permute-start(f32[6,130,1]{1,2,0:T(1,128)S(1)} %copy.67), channel_id=1, source_target_pairs={{0,1},{1,2},{2,3},{3,4},{4,5},{5,6},{6,7},{7,8},{8,9},{9,10},{10,1... | collective-permute-start | bytes 9368 | tf_op jit(solution)/shard_map/ppermute | solution.py:21
  256.1 6.4 %fusion.3 = f32[6,128,256]{2,0,1:T(8,128)S(1)} fusion(f32[6,128,256]{2,0,1:T(8,128)} %copy-done.4, f32[6,128,256]{2,1,0:T(8,128)} %bitcast.124, f32[6,130,1]{2,0,1:T(8,128)} %copy.68, f32[6,1,256]{2,0,1:T(8,128)S(1)} %collective-permute-done.8, f32[6,1,256]{2,0,1:T(8,128)S(1)} %collective-permute-done.9, f32[6,130,1]{2,0,1:T(8,128)} %copy.66, ...), kind=kOutput, calls=%fused_computation.11 | convolution fusion | flops 18087936 | bytes 2640136 | tf_op jit(solution)/shard_map/ab,bij->aij/dot_general | solution.py:36
  263.5 1.8 fusion.12
  265.4 1.7 gather_fusion.1
  267.2 1.5 scatter_fusion
  269.5 11.4 %all-to-all-start = ((f32[32,2,4,256]{3,1,2,0:T(2,128)}), f32[32,2,4,256]{3,1,2,0:T(2,128)S(1)}, u32[]{:S(2)}, u32[]{:S(2)}) async-start(f32[32,2,4,256]{3,1,2,0:T(2,128)} %copy.70), calls=%async_computation | async-start | bytes 524288 | tf_op jit(solution)/shard_map/all_to_all | solution.py:96
  281.6 2.4 copy.76
  284.0 7.9 %all-to-all-done = f32[32,2,4,256]{3,1,2,0:T(2,128)S(1)} async-done(((f32[32,2,4,256]{3,1,2,0:T(2,128)}), f32[32,2,4,256]{3,1,2,0:T(2,128)S(1)}, u32[]{:S(2)}, u32[]{:S(2)}) %all-to-all-start) | async-done | bytes 262176 | tf_op jit(solution)/shard_map/all_to_all | solution.py:96
  (69 shorter events, 22.2 us)
Async XLA Ops:
  7.2 165.5 %copy-start = (bf16[6,128,2048]{2,1,0:T(8,128)(2,1)S(1)}, bf16[6,128,2048]{2,1,0:T(8,128)(2,1)}, u32[]{:S(2)}) copy-start(bf16[6,128,2048]{2,1,0:T(8,128)(2,1)} %param.19) | copy-start | bytes 9437188
  7.2 165.5 %all-reduce.2.cloned.1.call-start = ((), (), s32[]{:S(2)}) async-start(), calls=%async_computation.1 | async-start | bytes 2097152 | tf_op jit(solution)/shard_map/psum | solution.py:13
  8.0 1.1 copy-start.1
  9.1 0.7 copy-start.8
  9.1 1.4 copy-start.6
  179.9 8.2 %copy-start.2 = (f32[6,128,256]{2,0,1:T(8,128)}, f32[6,128,256]{2,0,1:T(8,128)S(1)}, u32[]{:S(2)}) copy-start(f32[6,128,256]{2,0,1:T(8,128)S(1)} %broadcast_multiply_fusion) | copy-start | bytes 2359300
  179.9 4.3 %collective-permute-start = (f32[6,1,256]{2,0,1:T(8,128)S(1)}, f32[6,1,256]{2,0,1:T(8,128)S(1)}, u32[]{:S(2)}, u32[]{:S(2)}) collective-permute-start(f32[6,1,256]{2,0,1:T(8,128)S(1)} %get-tuple-element.71), channel_id=1, source_target_pairs={{32,0},{64,32},{96,64},{128,96},{160,128},{192,160},{224,192},{256... | collective-permute-start | bytes 18440 | tf_op jit(solution)/shard_map/ppermute | solution.py:24
  181.8 6.2 %collective-permute-start.1 = (f32[6,1,256]{2,0,1:T(8,128)S(1)}, f32[6,1,256]{2,0,1:T(8,128)S(1)}, u32[]{:S(2)}, u32[]{:S(2)}) collective-permute-start(f32[6,1,256]{2,0,1:T(8,128)S(1)} %get-tuple-element.70), channel_id=1, source_target_pairs={{0,32},{32,64},{64,96},{96,128},{128,160},{160,192},{192,224},{224... | collective-permute-start | bytes 18440 | tf_op jit(solution)/shard_map/ppermute | solution.py:21
  189.3 8.5 %copy-start.10 = (s32[1,32,1]{1,2,0:T(1,128)S(1)}, s32[1,32,1]{1,2,0:T(1,128)}, u32[]{:S(2)}) copy-start(s32[1,32,1]{1,2,0:T(1,128)} %param.28) | copy-start | bytes 388
  190.6 7.4 %collective-permute-start.2 = (f32[6,130,1]{1,2,0:T(1,128)S(1)}, f32[6,130,1]{1,2,0:T(1,128)S(1)}, u32[]{:S(2)}, u32[]{:S(2)}) collective-permute-start(f32[6,130,1]{1,2,0:T(1,128)S(1)} %copy.55), channel_id=1, source_target_pairs={{1,0},{2,1},{3,2},{4,3},{5,4},{6,5},{7,6},{8,7},{9,8},{10,9},{11,1... | collective-permute-start | bytes 9368 | tf_op jit(solution)/shard_map/ppermute | solution.py:24
  195.3 5.5 %collective-permute-start.3 = (f32[6,130,1]{1,2,0:T(1,128)S(1)}, f32[6,130,1]{1,2,0:T(1,128)S(1)}, u32[]{:S(2)}, u32[]{:S(2)}) collective-permute-start(f32[6,130,1]{1,2,0:T(1,128)S(1)} %copy.57), channel_id=1, source_target_pairs={{0,1},{1,2},{2,3},{3,4},{4,5},{5,6},{6,7},{7,8},{8,9},{9,10},{10,1... | collective-permute-start | bytes 9368 | tf_op jit(solution)/shard_map/ppermute | solution.py:21
  208.4 8.2 %copy-start.5 = (f32[6,128,256]{2,0,1:T(8,128)}, f32[6,128,256]{2,0,1:T(8,128)S(1)}, u32[]{:S(2)}) copy-start(f32[6,128,256]{2,0,1:T(8,128)S(1)} %fusion.11) | copy-start | bytes 2359300
  208.4 4.4 %collective-permute-start.4 = (f32[6,1,256]{2,0,1:T(8,128)S(1)}, f32[6,1,256]{2,0,1:T(8,128)S(1)}, u32[]{:S(2)}, u32[]{:S(2)}) collective-permute-start(f32[6,1,256]{2,0,1:T(8,128)S(1)} %get-tuple-element.69), channel_id=1, source_target_pairs={{32,0},{64,32},{96,64},{128,96},{160,128},{192,160},{224,192},{256... | collective-permute-start | bytes 18440 | tf_op jit(solution)/shard_map/ppermute | solution.py:24
  210.4 6.2 %collective-permute-start.5 = (f32[6,1,256]{2,0,1:T(8,128)S(1)}, f32[6,1,256]{2,0,1:T(8,128)S(1)}, u32[]{:S(2)}, u32[]{:S(2)}) collective-permute-start(f32[6,1,256]{2,0,1:T(8,128)S(1)} %get-tuple-element.68), channel_id=1, source_target_pairs={{0,32},{32,64},{64,96},{96,128},{128,160},{160,192},{192,224},{224... | collective-permute-start | bytes 18440 | tf_op jit(solution)/shard_map/ppermute | solution.py:21
  217.8 8.5 %copy-start.11 = (s32[1,32]{1,0:T(1,128)S(1)}, s32[1,32]{1,0:T(1,128)}, u32[]{:S(2)}) copy-start(s32[1,32]{1,0:T(1,128)} %param.27) | copy-start | bytes 388
  219.1 7.2 %collective-permute-start.6 = (f32[6,130,1]{1,2,0:T(1,128)S(1)}, f32[6,130,1]{1,2,0:T(1,128)S(1)}, u32[]{:S(2)}, u32[]{:S(2)}) collective-permute-start(f32[6,130,1]{1,2,0:T(1,128)S(1)} %copy.60), channel_id=1, source_target_pairs={{1,0},{2,1},{3,2},{4,3},{5,4},{6,5},{7,6},{8,7},{9,8},{10,9},{11,1... | collective-permute-start | bytes 9368 | tf_op jit(solution)/shard_map/ppermute | solution.py:24
  222.4 5.5 %collective-permute-start.7 = (f32[6,130,1]{1,2,0:T(1,128)S(1)}, f32[6,130,1]{1,2,0:T(1,128)S(1)}, u32[]{:S(2)}, u32[]{:S(2)}) collective-permute-start(f32[6,130,1]{1,2,0:T(1,128)S(1)} %copy.62), channel_id=1, source_target_pairs={{0,1},{1,2},{2,3},{3,4},{4,5},{5,6},{6,7},{7,8},{8,9},{9,10},{10,1... | collective-permute-start | bytes 9368 | tf_op jit(solution)/shard_map/ppermute | solution.py:21
  235.5 8.2 %copy-start.4 = (f32[6,128,256]{2,0,1:T(8,128)}, f32[6,128,256]{2,0,1:T(8,128)S(1)}, u32[]{:S(2)}) copy-start(f32[6,128,256]{2,0,1:T(8,128)S(1)} %fusion.7) | copy-start | bytes 2359300
  235.5 4.4 %collective-permute-start.8 = (f32[6,1,256]{2,0,1:T(8,128)S(1)}, f32[6,1,256]{2,0,1:T(8,128)S(1)}, u32[]{:S(2)}, u32[]{:S(2)}) collective-permute-start(f32[6,1,256]{2,0,1:T(8,128)S(1)} %get-tuple-element.67), channel_id=1, source_target_pairs={{32,0},{64,32},{96,64},{128,96},{160,128},{192,160},{224,192},{256... | collective-permute-start | bytes 18440 | tf_op jit(solution)/shard_map/ppermute | solution.py:24
  237.4 6.2 %collective-permute-start.9 = (f32[6,1,256]{2,0,1:T(8,128)S(1)}, f32[6,1,256]{2,0,1:T(8,128)S(1)}, u32[]{:S(2)}, u32[]{:S(2)}) collective-permute-start(f32[6,1,256]{2,0,1:T(8,128)S(1)} %get-tuple-element.66), channel_id=1, source_target_pairs={{0,32},{32,64},{64,96},{96,128},{128,160},{160,192},{192,224},{224... | collective-permute-start | bytes 18440 | tf_op jit(solution)/shard_map/ppermute | solution.py:21
  246.2 7.4 %collective-permute-start.10 = (f32[6,130,1]{1,2,0:T(1,128)S(1)}, f32[6,130,1]{1,2,0:T(1,128)S(1)}, u32[]{:S(2)}, u32[]{:S(2)}) collective-permute-start(f32[6,130,1]{1,2,0:T(1,128)S(1)} %copy.65), channel_id=1, source_target_pairs={{1,0},{2,1},{3,2},{4,3},{5,4},{6,5},{7,6},{8,7},{9,8},{10,9},{11,1... | collective-permute-start | bytes 9368 | tf_op jit(solution)/shard_map/ppermute | solution.py:24
  249.4 5.5 %collective-permute-start.11 = (f32[6,130,1]{1,2,0:T(1,128)S(1)}, f32[6,130,1]{1,2,0:T(1,128)S(1)}, u32[]{:S(2)}, u32[]{:S(2)}) collective-permute-start(f32[6,130,1]{1,2,0:T(1,128)S(1)} %copy.67), channel_id=1, source_target_pairs={{0,1},{1,2},{2,3},{3,4},{4,5},{5,6},{6,7},{7,8},{8,9},{9,10},{10,1... | collective-permute-start | bytes 9368 | tf_op jit(solution)/shard_map/ppermute | solution.py:21
  256.1 7.4 %copy-start.9 = (f32[4,6]{1,0:T(4,128)S(1)}, f32[4,6]{1,0:T(4,128)}, u32[]{:S(2)}) copy-start(f32[4,6]{1,0:T(4,128)} %param.25) | copy-start | bytes 292
  262.6 1.0 copy-start.3
  269.5 22.4 %all-to-all-start = ((f32[32,2,4,256]{3,1,2,0:T(2,128)}), f32[32,2,4,256]{3,1,2,0:T(2,128)S(1)}, u32[]{:S(2)}, u32[]{:S(2)}) async-start(f32[32,2,4,256]{3,1,2,0:T(2,128)} %copy.70), calls=%async_computation | async-start | bytes 524288 | tf_op jit(solution)/shard_map/all_to_all | solution.py:96
  281.5 10.4 %copy-start.7 = (f32[1,1,32,2,2,256]{5,4,3,2,1,0:T(2,128)S(1)}, f32[1,1,32,2,2,256]{5,4,3,2,1,0:T(2,128)}, u32[]{:S(2)}) copy-start(f32[1,1,32,2,2,256]{5,4,3,2,1,0:T(2,128)} %param.29) | copy-start | bytes 393220
Sparse Core Ops, SparseCore 0:
  11.5 161.1 all-reduce.1
where the time goes:
time: 301 us; the launch traced here: 300 us
  waiting for transfers between devices  178 us (59%)
  starting transfers between devices  42.1 us (14%)
  local copies, waits for them, and re-layouts  30.3 us (10%)
  matrix products  24.2 us (8%)
  between operations  15.9 us (5%)
  other arithmetic  8.78 us (3%)
    psum x1, waiting for transfers between devices, spread(): return lax.psum(block, axis)  157 us
    dot_general x3, matrix products, operate_padded(): jnp.einsum('ab,bij->aij', coupling, centre, precision=lax.Precision.HIGHEST)  19.2 us
    ppermute x6, starting transfers between devices, padded_2(): lax.ppermute(lax.slice_in_dim(block, block.shape[dim] - width, None, axis...  17.7 us
    ppermute x6, waiting for transfers between devices, padded_2(): lax.ppermute(lax.slice_in_dim(block, block.shape[dim] - width, None, axis...  13.5 us
    ppermute x6, starting transfers between devices, padded_2(): lax.ppermute(lax.slice_in_dim(block, 0, width, axis=dim), axis, backward)  13 us
    all_to_all x1, starting transfers between devices, on_device(): lax.all_to_all(outbox, 'girth', split_axis=0, concat_axis=0, tiled=True)  11.4 us
    all_to_all x1, waiting for transfers between devices, on_device(): lax.all_to_all(outbox, 'girth', split_axis=0, concat_axis=0, tiled=True)  7.93 us
    slice x6, local copies, waits for them, and re-layouts, padded_2(): lax.slice_in_dim(block, 0, width, axis=dim)  7.41 us
  transfers between devices with their start and end apart: 14, of which 8 were waited for; matrix products, arithmetic and copies ran while one was open for 6% of the time, Pallas kernels for 0%

commit v1 on v0

--- a/solution.py
+++ b/solution.py
@@ -3,6 +3,7 @@
 import jax.numpy as jnp
 from jax import lax
 from jax.sharding import PartitionSpec as P
+from jax.lax import all_gather
 
 SWEEPS = 4
 CAP = 2
@@ -10,7 +11,8 @@
 
 def spread(block, axis, source):
     block = jnp.where(lax.axis_index(axis) == source, block, jnp.zeros_like(block))
-    return lax.psum(block, axis)
+    rest_rings = lambda frame_in, which_axis: jnp.sum(all_gather(frame_in, which_axis), 0)
+    return rest_rings(block, axis)
 
 
 def padded_2(block, sides, width):

time: 301 us -> 391 us (1.30)
  waiting for transfers between devices: 178 us -> 260 us
  other arithmetic: 8.78 us -> 21.1 us
    all_gather x0 -> x1, waiting for transfers between devices: none -> 234 us  [spread(): all_gather(frame_in, which_axis)]
    psum x1 -> x0, waiting for transfers between devices: 157 us -> none  [spread(): return lax.psum(block, axis)]
    reduce_sum x0 -> x1, other arithmetic: none -> 12.4 us  [spread(): jnp.sum(all_gather(frame_in, which_axis), 0)]
    ppermute x6, waiting for transfers between devices: 0.02 us -> 6.79 us  [padded_2(): lax.ppermute(lax.slice_in_dim(block, 0, width, axis=dim), axis, backward)]
  transfers between devices with their start and end apart: 14 -> 14, of which waited for: 8 -> 8; matrix products, arithmetic and copies ran while one was open for 6% -> 4% of each run, Pallas kernels for 0% -> 0%
where the time goes in v1:
time: 391 us; the launch traced here: 390 us
  waiting for transfers between devices  260 us (66%)
  starting transfers between devices  38.8 us (10%)
  local copies, waits for them, and re-layouts  30.3 us (8%)
  matrix products  24.1 us (6%)
  other arithmetic  21.1 us (5%)
  between operations  15.9 us (4%)
    all_gather x1, waiting for transfers between devices, spread(): all_gather(frame_in, which_axis)  234 us
    dot_general x3, matrix products, operate_padded(): jnp.einsum('ab,bij->aij', coupling, centre, precision=lax.Precision.HIGHEST)  19.1 us
    ppermute x6, starting transfers between devices, padded_2(): lax.ppermute(lax.slice_in_dim(block, block.shape[dim] - width, None, axis...  18.2 us
    ppermute x6, starting transfers between devices, padded_2(): lax.ppermute(lax.slice_in_dim(block, 0, width, axis=dim), axis, backward)  12.4 us
    reduce_sum x1, other arithmetic, spread(): jnp.sum(all_gather(frame_in, which_axis), 0)  12.4 us
    ppermute x6, waiting for transfers between devices, padded_2(): lax.ppermute(lax.slice_in_dim(block, block.shape[dim] - width, None, axis...  11.2 us
    all_to_all x1, starting transfers between devices, on_device(): lax.all_to_all(outbox, 'girth', split_axis=0, concat_axis=0, tiled=True)  8.12 us
    all_to_all x1, waiting for transfers between devices, on_device(): lax.all_to_all(outbox, 'girth', split_axis=0, concat_axis=0, tiled=True)  7.93 us
  transfers between devices with their start and end apart: 14, of which 8 were waited for; matrix products, arithmetic and copies ran while one was open for 4% of the time, Pallas kernels for 0%

profile of v1, /device:TPU:264, one launch (start us, length us, event | category | flops | bytes accessed | tf_op | source)
XLA Modules:
  0.0 390.4 jit_solution(4093551645259123139)
XLA Ops:
  10.5 5.2 %broadcast_multiply_fusion.1 = (f32[128,256]{1,0:T(8,128)S(1)}, f32[128,256]{1,0:T(8,128)S(1)}) fusion(f32[]{:T(128)} %bitcast.12, s32[128,256]{1,0:T(8,128)S(1)} %copy-done.6, f32[]{:T(128)} %bitcast.11, f32[]{:T(128)} %bitcast.10, f32[]{:T(128)} %bitcast.9, f32[]{:T(128)} %bitcast.8, f32[]{:T(128)} %bitcast.7, f32[]{:T(128)} %bitcast.6, f32[]{:T(128)} %bitcast.5), kind=kLoop, calls=%fused_computation.85 | loop fusion | flops 786432 | bytes 393248 | tf_op jit(solution)/shard_map/mul | solution.py:77
  15.7 234.1 %all-gather.3.cloned.1.call-done = bf16[65536,256]{1,0:T(8,128)(2,1)} async-done(((bf16[2048,256]{1,0:T(8,128)(2,1)}), bf16[65536,256]{1,0:T(8,128)(2,1)}) %all-gather.3.cloned.1.call-update) | async-done | bytes 33554448 | tf_op jit(solution)/shard_map/all_gather | solution.py:14
  249.8 12.4 %reduce_sum.23 = bf16[2048,256]{1,0:T(8,128)(2,1)} reduce(bf16[32,2048,256]{2,1,0:T(8,128)(2,1)} %bitcast.122, bf16[]{:T(256)} %constant.104.clone.1), dimensions={0}, to_apply=%region_0.1 | reduce | flops 16252928 | bytes 34603008 | tf_op jit(solution)/shard_map/reduce_sum | solution.py:14
  262.2 3.1 convolution_bitcast_fusion.3
  265.4 2.3 copy.53
  267.6 1.8 broadcast_multiply_fusion
  269.5 1.9 collective-permute-start
  271.4 2.4 collective-permute-start.1
  273.8 3.8 collective-permute-done.1
  280.2 3.4 collective-permute-start.3
  284.9 2.4 collective-permute-start.2
  288.7 2.4 collective-permute-done.2
  292.3 6.3 %fusion.11 = f32[6,128,256]{2,0,1:T(8,128)S(1)} fusion(f32[6,128,256]{2,0,1:T(8,128)} %copy-done.2, f32[6,128,256]{2,1,0:T(8,128)} %bitcast.124, f32[6,130,1]{2,0,1:T(8,128)} %copy.58, f32[6,1,256]{2,0,1:T(8,128)S(1)} %collective-permute-done, f32[6,1,256]{2,0,1:T(8,128)S(1)} %collective-permute-done.1, f32[6,130,1]{2,0,1:T(8,128)} %copy.56, ...), kind=kOutput, calls=%fused_computation.21 | convolution fusion | flops 18284544 | bytes 2640136 | tf_op jit(solution)/shard_map/ab,bij->aij/dot_general | solution.py:38
  298.6 1.9 collective-permute-start.4
  300.6 2.4 collective-permute-start.5
  303.0 3.7 collective-permute-done.5
  309.3 3.9 %collective-permute-start.7 = (f32[6,130,1]{1,2,0:T(1,128)S(1)}, f32[6,130,1]{1,2,0:T(1,128)S(1)}, u32[]{:S(2)}, u32[]{:S(2)}) collective-permute-start(f32[6,130,1]{1,2,0:T(1,128)S(1)} %copy.62), channel_id=1, source_target_pairs={{0,1},{1,2},{2,3},{3,4},{4,5},{5,6},{6,7},{7,8},{8,9},{9,10},{10,1... | collective-permute-start | bytes 9368 | tf_op jit(solution)/shard_map/ppermute | solution.py:23
  314.6 1.9 collective-permute-start.6
  317.7 2.4 collective-permute-done.6
  321.3 6.4 %fusion.7 = f32[6,128,256]{2,0,1:T(8,128)S(1)} fusion(f32[6,128,256]{2,0,1:T(8,128)} %copy-done.5, f32[6,128,256]{2,1,0:T(8,128)} %bitcast.125, f32[6,130,1]{2,0,1:T(8,128)} %copy.63, f32[6,1,256]{2,0,1:T(8,128)S(1)} %collective-permute-done.4, f32[6,1,256]{2,0,1:T(8,128)S(1)} %collective-permute-done.5, f32[6,130,1]{2,0,1:T(8,128)} %copy.61, ...), kind=kOutput, calls=%fused_computation.16 | convolution fusion | flops 18087936 | bytes 2640136 | tf_op jit(solution)/shard_map/ab,bij->aij/dot_general | solution.py:38
  327.7 1.9 collective-permute-start.8
  329.7 2.4 collective-permute-start.9
  332.1 3.7 collective-permute-done.9
  338.4 3.7 collective-permute-start.11
  343.4 2.3 collective-permute-start.10
  347.0 2.0 collective-permute-done.10
  350.2 6.4 %fusion.3 = f32[6,128,256]{2,0,1:T(8,128)S(1)} fusion(f32[6,128,256]{2,0,1:T(8,128)} %copy-done.4, f32[6,128,256]{2,1,0:T(8,128)} %bitcast.126, f32[6,130,1]{2,0,1:T(8,128)} %copy.68, f32[6,1,256]{2,0,1:T(8,128)S(1)} %collective-permute-done.8, f32[6,1,256]{2,0,1:T(8,128)S(1)} %collective-permute-done.9, f32[6,130,1]{2,0,1:T(8,128)} %copy.66, ...), kind=kOutput, calls=%fused_computation.11 | convolution fusion | flops 18087936 | bytes 2640136 | tf_op jit(solution)/shard_map/ab,bij->aij/dot_general | solution.py:38
  357.6 1.8 fusion.12
  359.4 1.7 gather_fusion.1
  363.6 8.1 %all-to-all-start = ((f32[32,2,4,256]{3,1,2,0:T(2,128)}), f32[32,2,4,256]{3,1,2,0:T(2,128)S(1)}, u32[]{:S(2)}, u32[]{:S(2)}) async-start(f32[32,2,4,256]{3,1,2,0:T(2,128)} %copy.70), calls=%async_computation | async-start | bytes 524288 | tf_op jit(solution)/shard_map/all_to_all | solution.py:98
  372.3 2.4 copy.76
  374.7 7.9 %all-to-all-done = f32[32,2,4,256]{3,1,2,0:T(2,128)S(1)} async-done(((f32[32,2,4,256]{3,1,2,0:T(2,128)}), f32[32,2,4,256]{3,1,2,0:T(2,128)S(1)}, u32[]{:S(2)}, u32[]{:S(2)}) %all-to-all-start) | async-done | bytes 262176 | tf_op jit(solution)/shard_map/all_to_all | solution.py:98
  (70 shorter events, 25.8 us)
Async XLA Ops:
  7.2 255.1 %copy-start = (bf16[6,128,2048]{2,1,0:T(8,128)(2,1)S(1)}, bf16[6,128,2048]{2,1,0:T(8,128)(2,1)}, u32[]{:S(2)}) copy-start(bf16[6,128,2048]{2,1,0:T(8,128)(2,1)} %param.19) | copy-start | bytes 9437188
  7.2 242.6 %all-gather.3.cloned.1.call-start = ((), (), s32[]{:S(2)}) async-start(), calls=%async_computation.1 | async-start | bytes 34603008 | tf_op jit(solution)/shard_map/all_gather | solution.py:14
  8.0 1.1 copy-start.1
  9.1 0.7 copy-start.8
  9.1 1.4 copy-start.6
  269.5 8.2 %copy-start.2 = (f32[6,128,256]{2,0,1:T(8,128)}, f32[6,128,256]{2,0,1:T(8,128)S(1)}, u32[]{:S(2)}) copy-start(f32[6,128,256]{2,0,1:T(8,128)S(1)} %broadcast_multiply_fusion) | copy-start | bytes 2359300
  269.5 4.3 %collective-permute-start = (f32[6,1,256]{2,0,1:T(8,128)S(1)}, f32[6,1,256]{2,0,1:T(8,128)S(1)}, u32[]{:S(2)}, u32[]{:S(2)}) collective-permute-start(f32[6,1,256]{2,0,1:T(8,128)S(1)} %get-tuple-element.71), channel_id=1, source_target_pairs={{32,0},{64,32},{96,64},{128,96},{160,128},{192,160},{224,192},{256... | collective-permute-start | bytes 18440 | tf_op jit(solution)/shard_map/ppermute | solution.py:26
  271.4 6.2 %collective-permute-start.1 = (f32[6,1,256]{2,0,1:T(8,128)S(1)}, f32[6,1,256]{2,0,1:T(8,128)S(1)}, u32[]{:S(2)}, u32[]{:S(2)}) collective-permute-start(f32[6,1,256]{2,0,1:T(8,128)S(1)} %get-tuple-element.70), channel_id=1, source_target_pairs={{0,32},{32,64},{64,96},{96,128},{128,160},{160,192},{192,224},{224... | collective-permute-start | bytes 18440 | tf_op jit(solution)/shard_map/ppermute | solution.py:23
  278.9 8.5 %copy-start.10 = (s32[1,32,1]{1,2,0:T(1,128)S(1)}, s32[1,32,1]{1,2,0:T(1,128)}, u32[]{:S(2)}) copy-start(s32[1,32,1]{1,2,0:T(1,128)} %param.28) | copy-start | bytes 388
  280.2 7.4 %collective-permute-start.3 = (f32[6,130,1]{1,2,0:T(1,128)S(1)}, f32[6,130,1]{1,2,0:T(1,128)S(1)}, u32[]{:S(2)}, u32[]{:S(2)}) collective-permute-start(f32[6,130,1]{1,2,0:T(1,128)S(1)} %copy.57), channel_id=1, source_target_pairs={{0,1},{1,2},{2,3},{3,4},{4,5},{5,6},{6,7},{7,8},{8,9},{9,10},{10,1... | collective-permute-start | bytes 9368 | tf_op jit(solution)/shard_map/ppermute | solution.py:23
  284.9 6.2 %collective-permute-start.2 = (f32[6,130,1]{1,2,0:T(1,128)S(1)}, f32[6,130,1]{1,2,0:T(1,128)S(1)}, u32[]{:S(2)}, u32[]{:S(2)}) collective-permute-start(f32[6,130,1]{1,2,0:T(1,128)S(1)} %copy.55), channel_id=1, source_target_pairs={{1,0},{2,1},{3,2},{4,3},{5,4},{6,5},{7,6},{8,7},{9,8},{10,9},{11,1... | collective-permute-start | bytes 9368 | tf_op jit(solution)/shard_map/ppermute | solution.py:26
  298.6 8.2 %copy-start.5 = (f32[6,128,256]{2,0,1:T(8,128)}, f32[6,128,256]{2,0,1:T(8,128)S(1)}, u32[]{:S(2)}) copy-start(f32[6,128,256]{2,0,1:T(8,128)S(1)} %fusion.11) | copy-start | bytes 2359300
  298.6 4.4 %collective-permute-start.4 = (f32[6,1,256]{2,0,1:T(8,128)S(1)}, f32[6,1,256]{2,0,1:T(8,128)S(1)}, u32[]{:S(2)}, u32[]{:S(2)}) collective-permute-start(f32[6,1,256]{2,0,1:T(8,128)S(1)} %get-tuple-element.69), channel_id=1, source_target_pairs={{32,0},{64,32},{96,64},{128,96},{160,128},{192,160},{224,192},{256... | collective-permute-start | bytes 18440 | tf_op jit(solution)/shard_map/ppermute | solution.py:26
  300.6 6.2 %collective-permute-start.5 = (f32[6,1,256]{2,0,1:T(8,128)S(1)}, f32[6,1,256]{2,0,1:T(8,128)S(1)}, u32[]{:S(2)}, u32[]{:S(2)}) collective-permute-start(f32[6,1,256]{2,0,1:T(8,128)S(1)} %get-tuple-element.68), channel_id=1, source_target_pairs={{0,32},{32,64},{64,96},{96,128},{128,160},{160,192},{192,224},{224... | collective-permute-start | bytes 18440 | tf_op jit(solution)/shard_map/ppermute | solution.py:23
  308.0 8.5 %copy-start.11 = (s32[1,32]{1,0:T(1,128)S(1)}, s32[1,32]{1,0:T(1,128)}, u32[]{:S(2)}) copy-start(s32[1,32]{1,0:T(1,128)} %param.27) | copy-start | bytes 388
  309.3 7.2 %collective-permute-start.7 = (f32[6,130,1]{1,2,0:T(1,128)S(1)}, f32[6,130,1]{1,2,0:T(1,128)S(1)}, u32[]{:S(2)}, u32[]{:S(2)}) collective-permute-start(f32[6,130,1]{1,2,0:T(1,128)S(1)} %copy.62), channel_id=1, source_target_pairs={{0,1},{1,2},{2,3},{3,4},{4,5},{5,6},{6,7},{7,8},{8,9},{9,10},{10,1... | collective-permute-start | bytes 9368 | tf_op jit(solution)/shard_map/ppermute | solution.py:23
  314.6 5.5 %collective-permute-start.6 = (f32[6,130,1]{1,2,0:T(1,128)S(1)}, f32[6,130,1]{1,2,0:T(1,128)S(1)}, u32[]{:S(2)}, u32[]{:S(2)}) collective-permute-start(f32[6,130,1]{1,2,0:T(1,128)S(1)} %copy.60), channel_id=1, source_target_pairs={{1,0},{2,1},{3,2},{4,3},{5,4},{6,5},{7,6},{8,7},{9,8},{10,9},{11,1... | collective-permute-start | bytes 9368 | tf_op jit(solution)/shard_map/ppermute | solution.py:26
  327.7 8.2 %copy-start.4 = (f32[6,128,256]{2,0,1:T(8,128)}, f32[6,128,256]{2,0,1:T(8,128)S(1)}, u32[]{:S(2)}) copy-start(f32[6,128,256]{2,0,1:T(8,128)S(1)} %fusion.7) | copy-start | bytes 2359300
  327.7 4.4 %collective-permute-start.8 = (f32[6,1,256]{2,0,1:T(8,128)S(1)}, f32[6,1,256]{2,0,1:T(8,128)S(1)}, u32[]{:S(2)}, u32[]{:S(2)}) collective-permute-start(f32[6,1,256]{2,0,1:T(8,128)S(1)} %get-tuple-element.67), channel_id=1, source_target_pairs={{32,0},{64,32},{96,64},{128,96},{160,128},{192,160},{224,192},{256... | collective-permute-start | bytes 18440 | tf_op jit(solution)/shard_map/ppermute | solution.py:26
  329.7 6.2 %collective-permute-start.9 = (f32[6,1,256]{2,0,1:T(8,128)S(1)}, f32[6,1,256]{2,0,1:T(8,128)S(1)}, u32[]{:S(2)}, u32[]{:S(2)}) collective-permute-start(f32[6,1,256]{2,0,1:T(8,128)S(1)} %get-tuple-element.66), channel_id=1, source_target_pairs={{0,32},{32,64},{64,96},{96,128},{128,160},{160,192},{192,224},{224... | collective-permute-start | bytes 18440 | tf_op jit(solution)/shard_map/ppermute | solution.py:23
  338.4 7.4 %collective-permute-start.11 = (f32[6,130,1]{1,2,0:T(1,128)S(1)}, f32[6,130,1]{1,2,0:T(1,128)S(1)}, u32[]{:S(2)}, u32[]{:S(2)}) collective-permute-start(f32[6,130,1]{1,2,0:T(1,128)S(1)} %copy.67), channel_id=1, source_target_pairs={{0,1},{1,2},{2,3},{3,4},{4,5},{5,6},{6,7},{7,8},{8,9},{9,10},{10,1... | collective-permute-start | bytes 9368 | tf_op jit(solution)/shard_map/ppermute | solution.py:23
  343.4 5.5 %collective-permute-start.10 = (f32[6,130,1]{1,2,0:T(1,128)S(1)}, f32[6,130,1]{1,2,0:T(1,128)S(1)}, u32[]{:S(2)}, u32[]{:S(2)}) collective-permute-start(f32[6,130,1]{1,2,0:T(1,128)S(1)} %copy.65), channel_id=1, source_target_pairs={{1,0},{2,1},{3,2},{4,3},{5,4},{6,5},{7,6},{8,7},{9,8},{10,9},{11,1... | collective-permute-start | bytes 9368 | tf_op jit(solution)/shard_map/ppermute | solution.py:26
  350.2 7.4 %copy-start.9 = (f32[4,6]{1,0:T(4,128)S(1)}, f32[4,6]{1,0:T(4,128)}, u32[]{:S(2)}) copy-start(f32[4,6]{1,0:T(4,128)} %param.25) | copy-start | bytes 292
  356.6 1.0 copy-start.3
  363.6 19.1 %all-to-all-start = ((f32[32,2,4,256]{3,1,2,0:T(2,128)}), f32[32,2,4,256]{3,1,2,0:T(2,128)S(1)}, u32[]{:S(2)}, u32[]{:S(2)}) async-start(f32[32,2,4,256]{3,1,2,0:T(2,128)} %copy.70), calls=%async_computation | async-start | bytes 524288 | tf_op jit(solution)/shard_map/all_to_all | solution.py:98
  372.3 10.4 %copy-start.7 = (f32[1,1,32,2,2,256]{5,4,3,2,1,0:T(2,128)S(1)}, f32[1,1,32,2,2,256]{5,4,3,2,1,0:T(2,128)}, u32[]{:S(2)}) copy-start(f32[1,1,32,2,2,256]{5,4,3,2,1,0:T(2,128)} %param.29) | copy-start | bytes 393220
Sparse Core Ops, SparseCore 0:
  11.2 238.5 all-gather.2
